TPU v7x, 256 devices: a whole 4x4x8 slice. The times are simulated.
256 devices in a mesh: grp: 32 (over z, y_hi, core), tp: 8 (over y_lo, x).
Axes of the slice: x: 4, y: 4 (y_hi: 2, y_lo: 2; y = y_hi * 2 + y_lo), z: 8, core: 2. Of those that a mesh axis runs over, the one named last changes fastest.
Arguments:
- states_in: bfloat16 [16384, 1536], P('grp', 'tp'), may hold values from -6 to 6
- segment_ids: int32 [16384], P('grp'), may hold values from 0 to 223, as said below
- positions: int32 [16384], P('grp'), may hold values from 0 to 1009, as said below
- attention_gain: bfloat16 [1536], P('tp'), may hold values from 0.5 to 1.5
- feedforward_gain: bfloat16 [1536], P('tp'), may hold values from 0.5 to 1.5
- query_weight: bfloat16 [1536, 1536], P('grp', 'tp'), may hold values from -1 to 1
- keyvalue_weight: bfloat16 [1536, 8, 128], P('grp', 'tp'), may hold values from -128 to 128
- output_weight: bfloat16 [1536, 1536], P('tp'), may hold values from -0.15625 to 0.15625
- route_experts: int32 [16384, 8], P('grp'), may hold values from 0 to 19, all different within a row; in each aligned block of 512 rows (0 to 511, 512 to 1023, ...) at most 256 rows name the same one
- route_weights: float32 [16384, 8], P('grp'), may hold values from 0.05 to 0.3
- expert_gateup: bfloat16 [40, 1536, 512], P('tp'), may hold values from -0.15625 to 0.15625
- expert_down: bfloat16 [40, 256, 1536], P('tp'), may hold values from -0.25 to 0.25
- cache_slots: int32 [16384], P('grp'), may hold values from 0 to 16383, as said below
Outputs:
- layer_output: bfloat16 [16384, 1536], P('grp', 'tp')
- paged_cache: bfloat16 [16384, 8, 128], P('grp', 'tp')
- log_sums: float32 [24, 16384], P('tp', 'grp')
Inputs may be any that keep to these rules, and one draw needn't show every extreme that they name: `segment_ids`: equal ids mark the tokens of one prompt; the tokens of a prompt lie within one pair of groups 2p and 2p+1. `positions`: positions count from 0 within each prompt; one prompt of groups 0 and 1 has 2 * (505) tokens. `route_experts`: each row names 8 different experts; at most 256 rows of one group name the same expert, and that number is reached. `cache_slots`: every cache row is named once; the tokens of each group fill exactly 16 rows of every group's block of 512 rows.
All inputs are finite; a program needn't handle non-finite values.
Results may differ from a plain program's by a relative error of at most 0.01.
The roundings to bfloat16 on the way count: a program that leaves them out, or rounds other values in their place, can miss the bound.
Values may be sent and summed in bfloat16 or wider, within the bound.
No kernel may reach another device: no remote copies, remote signals or barrier semaphores. Data moves between devices by JAX's collectives and lax.ppermute only.
A program may use at most 128 MiB of HBM per device.

v0:
```python
import jax
import jax.numpy as jnp
from jax import lax
from jax.sharding import Mesh
from jax.sharding import PartitionSpec as P

HD = 64
attn_scale = 0.015625
norm_eps = 1e-06
rope_base = 10000.0
G = ("z", "yh", "c")
T = ("yl", "x")


def rms_scale(values, gain_row):
    floats = values.astype(jnp.float32)
    mean_square = jnp.mean(floats * floats, axis=-1, keepdims=True)
    return (floats * lax.rsqrt(mean_square + norm_eps) * gain_row.astype(jnp.float32)).astype(
        jnp.bfloat16
    )


def rotate(values, places):
    half_width = values.shape[-1] // 2
    frequency = rope_base ** (-jnp.arange(half_width, dtype=jnp.float32) * 2.0 / values.shape[-1])
    angles = places.astype(jnp.float32)[:, None] * frequency[None, :]
    cosine = jnp.cos(angles)[:, None, :]
    sine_part = jnp.sin(angles)[:, None, :]
    leading = values[..., :half_width]
    trailing = values[..., half_width:]
    return jnp.concatenate(
        [leading * cosine - trailing * sine_part, trailing * cosine + leading * sine_part], axis=-1
    )


def attend_block(query_block, seg_block, pos_block, all_rows, all_seg, all_pos):
    key_part = all_rows[..., :HD]
    value_part = all_rows[..., HD:]
    scores = (
        jnp.einsum("qgrd,kgd->grqk", query_block, key_part, preferred_element_type=jnp.float32)
        * attn_scale
    )
    allowed = (seg_block[:, None] == all_seg[None, :]) & (all_pos[None, :] <= pos_block[:, None])
    masked = jnp.where(allowed, scores, -jnp.inf)
    row_peak = jnp.max(masked, axis=-1, keepdims=True)
    exponent = jnp.exp(masked - row_peak)
    row_total = jnp.sum(exponent, axis=-1, keepdims=True)
    log_total = (row_peak + jnp.log(row_total))[..., 0]
    weights_low = (exponent / row_total).astype(jnp.bfloat16)
    mixed_rows = jnp.einsum(
        "grqk,kgd->qgrd", weights_low, value_part, preferred_element_type=jnp.float32
    )
    return (mixed_rows.astype(jnp.bfloat16), log_total)


def expert_terms(normed, route_experts, route_weights, gateup, down, slot_first):
    local_experts = gateup.shape[0]
    half_units = down.shape[1]
    owned_experts = slot_first + jnp.arange(local_experts, dtype=jnp.int32)
    matches = route_experts[:, :, None] == owned_experts[None, None, :]
    route_scale = jnp.sum(jnp.where(matches, route_weights[:, :, None], 0.0), axis=1)
    gate_up = jnp.einsum("td,edf->etf", normed, gateup, preferred_element_type=jnp.float32)
    activated = (jax.nn.silu(gate_up[..., :half_units]) * gate_up[..., half_units:]).astype(
        jnp.bfloat16
    )
    produced = jnp.einsum("etf,efd->etd", activated, down, preferred_element_type=jnp.float32)
    return jnp.sum(route_scale.T[:, :, None] * produced, axis=0)


def gather_rows_over_groups(block):
    width = block.shape[1]
    nz = lax.axis_size("z")
    zi = lax.axis_index("z")
    got = [block]
    for k in range(1, nz):
        got.append(lax.ppermute(block, "z", [(i, (i + k) % nz) for i in range(nz)]))
    stacked = jnp.stack(got)
    zfull = jnp.take(stacked, (zi - jnp.arange(nz)) % nz, axis=0)
    yi = lax.axis_index("yh")
    other_y = lax.ppermute(zfull, "yh", [(0, 1), (1, 0)])
    yfull = jnp.where(yi == 0, jnp.stack([zfull, other_y]), jnp.stack([other_y, zfull]))
    ci = lax.axis_index("c")
    other_c = lax.ppermute(yfull, "c", [(0, 1), (1, 0)])
    cfull = jnp.where(ci == 0, jnp.stack([yfull, other_c]), jnp.stack([other_c, yfull]))
    return cfull.transpose(2, 1, 0, 3, 4).reshape(-1, width)


def shards(
    states_in,
    segment_ids,
    positions,
    attention_gain,
    feedforward_gain,
    query_weight,
    keyvalue_weight,
    output_weight,
    route_experts,
    route_weights,
    expert_gateup,
    expert_down,
    cache_slots,
):
    tokens = states_in.shape[0]
    width_share = states_in.shape[1]
    head_rank = lax.axis_index(T)
    group_rank = lax.axis_index(G)
    gain_rows = jnp.zeros((8, width_share), states_in.dtype)
    gain_rows = gain_rows.at[0].set(attention_gain).at[1].set(feedforward_gain)
    packed = jnp.concatenate([states_in, gain_rows], axis=0)
    packed_full = lax.all_gather(packed, T, axis=1, tiled=True)
    states_full = packed_full[:tokens]
    gain_attend = packed_full[tokens]
    gain_forward = packed_full[tokens + 1]
    normed_in = rms_scale(states_full, gain_attend)
    query_cols = query_weight.shape[1]
    keyvalue_heads = keyvalue_weight.shape[1]
    heads_local = query_cols // HD
    piece_rows = query_weight.shape[0]
    weights_packed = jnp.concatenate(
        [query_weight, keyvalue_weight.reshape(piece_rows, -1)], axis=1
    )
    weights_full = gather_rows_over_groups(weights_packed)
    query_full_w = weights_full[:, :query_cols]
    keyvalue_full_w = weights_full[:, query_cols:]
    query_sum = jnp.dot(normed_in, query_full_w, preferred_element_type=jnp.float32)
    keyvalue_sum = jnp.dot(normed_in, keyvalue_full_w, preferred_element_type=jnp.float32)
    queries = rotate(query_sum.reshape(tokens, heads_local, HD), positions).astype(jnp.bfloat16)
    keyvalue_sum = keyvalue_sum.reshape(tokens, keyvalue_heads, 2 * HD)
    key_rows = rotate(keyvalue_sum[..., :HD], positions).astype(jnp.bfloat16)
    value_rows = keyvalue_sum[..., HD:].astype(jnp.bfloat16)
    own_rows = jnp.concatenate([key_rows, value_rows], axis=-1)
    other_rows, other_seg, other_pos = lax.ppermute(
        (own_rows, segment_ids, positions), "c", [(0, 1), (1, 0)]
    )
    all_rows = jnp.concatenate([own_rows, other_rows], axis=0)
    all_seg = jnp.concatenate([segment_ids, other_seg], axis=0)
    all_pos = jnp.concatenate([positions, other_pos], axis=0)
    group_ratio = heads_local // keyvalue_heads
    query_block = queries.reshape(tokens, keyvalue_heads, group_ratio, HD)
    mixed, log_part = attend_block(query_block, segment_ids, positions, all_rows, all_seg, all_pos)
    attended = mixed.reshape(tokens, heads_local * HD)
    log_sums = log_part.reshape(heads_local, tokens)
    partial_value = jnp.dot(attended, output_weight, preferred_element_type=jnp.float32)
    summed = lax.psum(partial_value, T)
    residual = (states_full.astype(jnp.float32) + summed).astype(jnp.bfloat16)
    normed = rms_scale(residual, gain_forward)
    residual_share = lax.dynamic_slice_in_dim(residual, head_rank * width_share, width_share, 1)
    slot_first = head_rank // 2 * expert_gateup.shape[0]
    terms = expert_terms(
        normed, route_experts, route_weights, expert_gateup, expert_down, slot_first
    )
    expert_share = lax.psum_scatter(
        terms.astype(jnp.bfloat16), T, scatter_dimension=1, tiled=True
    ).astype(jnp.float32)
    layer_output = (residual_share.astype(jnp.float32) + expert_share).astype(jnp.bfloat16)
    group_count = lax.axis_size(G)
    per_owner = tokens // group_count
    owners = cache_slots // tokens
    sequence = jnp.arange(tokens, dtype=jnp.int32)
    ordering = jnp.argsort(owners * tokens + sequence)
    send_rows = own_rows[ordering].reshape(group_count, per_owner, keyvalue_heads, 2 * HD)
    send_slots = cache_slots[ordering].reshape(group_count, per_owner)
    got_rows, got_slots = (
        lax.all_to_all(send_rows, G, split_axis=0, concat_axis=0, tiled=True),
        lax.all_to_all(send_slots, G, split_axis=0, concat_axis=0, tiled=True),
    )
    targets = got_slots.reshape(tokens) - group_rank * tokens
    paged_rows = (
        jnp.zeros_like(own_rows).at[targets].set(got_rows.reshape(tokens, keyvalue_heads, 2 * HD))
    )
    return (layer_output, paged_rows, log_sums)


def solution(mesh):
    fine = Mesh(mesh.devices.reshape(8, 2, 2, 2, 4), ("z", "yh", "c", "yl", "x"))
    return jax.shard_map(
        shards,
        mesh=fine,
        in_specs=(
            P(G, T),
            P(G),
            P(G),
            P(T),
            P(T),
            P(G, T),
            P(G, T, None),
            P(T, None),
            P(G, None),
            P(G, None),
            P(T, None, None),
            P(T, None, None),
            P(G),
        ),
        out_specs=(P(G, T), P(G, T, None), P(T, G)),
        check_vma=False,
    )
```

profile of v0, /device:TPU:1, one launch (start us, length us, event | category | flops | bytes accessed | tf_op | source)
XLA Modules:
  0.0 252.0 jit_solution(752531297667724004)
XLA Ops:
  8.1 2.5 collective-permute-start
  10.6 3.0 %collective-permute-start.1 = (bf16[48,320]{1,0:T(8,128)(2,1)S(1)}, bf16[48,320]{1,0:T(8,128)(2,1)S(1)}, u32[]{:S(2)}, u32[]{:S(2)}) collective-permute-start(bf16[48,320]{1,0:T(8,128)(2,1)S(1)} %pad_maximum_fusion.3), channel_id=1, source_target_pairs={{0,64},{32,96},{64,128},{96,160},{128,192},{160,224},{192,0},{224,... | collective-permute-start | bytes 92168 | tf_op jit(solution)/shard_map/ppermute | solution.py:76
  13.6 3.8 %collective-permute-start.2 = (bf16[48,320]{1,0:T(8,128)(2,1)S(1)}, bf16[48,320]{1,0:T(8,128)(2,1)S(1)}, u32[]{:S(2)}, u32[]{:S(2)}) collective-permute-start(bf16[48,320]{1,0:T(8,128)(2,1)S(1)} %pad_maximum_fusion.3), channel_id=1, source_target_pairs={{0,96},{32,128},{64,160},{96,192},{128,224},{160,0},{192,32},{224,... | collective-permute-start | bytes 92168 | tf_op jit(solution)/shard_map/ppermute | solution.py:76
  19.3 1.7 pad_maximum_fusion.1
  21.1 1.7 collective-permute-start.10
  24.7 4.7 %collective-permute-start.4 = (bf16[48,320]{1,0:T(8,128)(2,1)S(1)}, bf16[48,320]{1,0:T(8,128)(2,1)S(1)}, u32[]{:S(2)}, u32[]{:S(2)}) collective-permute-start(bf16[48,320]{1,0:T(8,128)(2,1)S(1)} %pad_maximum_fusion.3), channel_id=1, source_target_pairs={{0,160},{32,192},{64,224},{96,0},{128,32},{160,64},{192,96},{224,1... | collective-permute-start | bytes 92168 | tf_op jit(solution)/shard_map/ppermute | solution.py:76
  30.1 2.5 collective-permute-start.5
  36.2 3.0 %collective-permute-start.7 = (bf16[8,48,320]{2,1,0:T(8,128)(2,1)S(1)}, bf16[8,48,320]{2,1,0:T(8,128)(2,1)S(1)}, u32[]{:S(2)}, u32[]{:S(2)}) collective-permute-start(bf16[8,48,320]{2,1,0:T(8,128)(2,1)S(1)} %broadcast_select_fusion), channel_id=1, source_target_pairs={{0,16},{16,0},{1,17},{17,1},{2,18},{18,2},{3,19},{19,3},{4,20},{20... | collective-permute-start | bytes 737288 | tf_op jit(solution)/shard_map/ppermute | solution.py:80
  40.0 23.9 %collective-permute-done.7 = bf16[8,48,320]{2,1,0:T(8,128)(2,1)S(1)} collective-permute-done((bf16[8,48,320]{2,1,0:T(8,128)(2,1)S(1)}, bf16[8,48,320]{2,1,0:T(8,128)(2,1)S(1)}, u32[]{:S(2)}, u32[]{:S(2)}) %collective-permute-start.7) | collective-permute-done | bytes 245792 | tf_op jit(solution)/shard_map/ppermute | solution.py:80
  66.8 1.1 copy.50
  68.0 2.6 %slice.95 = bf16[512,1536]{0,1:T(8,128)(2,1)} slice(bf16[520,1536]{0,1:T(8,128)(2,1)} %all-gather.2.cloned.1.call-done), slice={[0:512], [0:1536]} | slice | bytes 3145728 | tf_op jit(solution)/shard_map/slice | solution.py:111
  70.6 1.7 copy.59
  72.7 1.5 convert_reduce_fusion
  74.3 2.0 convolution_bitcast_fusion.1
  78.9 1.3 fusion.1
  80.2 1.4 fusion
  81.6 2.0 fusion.19
  83.7 2.3 fusion.54
  86.5 91.7 %all-reduce.3.cloned.1.call-done = f32[512,1536]{1,0:T(8,128)} async-done(((f32[512,1536]{1,0:T(8,128)}), f32[512,1536]{1,0:T(8,128)}) %all-reduce.3.cloned.1.call-update) | async-done | bytes 3145744 | tf_op jit(solution)/shard_map/psum | solution.py:144
  178.2 2.4 fusion.2
  180.6 7.5 %convolution_bitcast_fusion = f32[5,512,512]{2,1,0:T(8,128)S(1)} fusion(bf16[5,1536,512]{2,1,0:T(8,128)(2,1)} %param.27, bf16[512,1536]{1,0:T(8,128)(2,1)S(1)} %get-tuple-element.47, f32[1536]{0:T(1024)S(1)} %get-tuple-element.44, f32[512]{0:T(512)S(1)} %add_rsqrt_fusion), kind=kOutput, calls=%fused_computation.26 | convolution fusion | flops 4029677568 | bytes 14688256 | tf_op jit(solution)/shard_map/td,edf->etf/dot_general | solution.py:62
  188.2 3.5 %multiply_reduce_fusion = bf16[512,1536]{1,0:T(8,128)(2,1)S(1)} fusion(bf16[5,256,1536]{2,1,0:T(8,128)(2,1)S(1)} %copy-done.8, f32[5,512]{1,0:T(8,128)S(1)} %bitcast.103, f32[5,512,512]{2,1,0:T(8,128)S(1)} %convolution_bitcast_fusion), kind=kOutput, calls=%fused_computation.4 | convolution fusion | flops 2024275968 | bytes 10758144 | tf_op jit(solution)/shard_map/etf,efd->etd/dot_general | solution.py:66
  191.7 1.6 copy.57
  193.3 3.8 %sort.17 = (s32[512]{0:T(512)}, s32[512]{0:T(512)S(1)}) sort(s32[512]{0:T(512)S(1)} %fusion.43, s32[512]{0:T(512)S(1)} %iota.31), dimensions={0}, to_apply=%region_8.9 | sort | flops 4608 | bytes 8192 | tf_op jit(solution)/shard_map/jit(argsort)/sort | solution.py:160
  197.1 3.5 %gather_fusion.1 = s32[512]{0:T(512)S(1)} fusion(s32[512]{0:T(512)S(1)} %copy-done.1, s32[1024]{0:T(1024)S(1)} %pad_clamp_fusion), kind=kCustom, calls=%fused_computation.1 | custom fusion | bytes 6144 | tf_op jit(solution)/shard_map/gather | solution.py:162
  201.3 12.2 %all-to-all-start = ((s32[32,1,16]{2,1,0:T(1,128)}), s32[32,1,16]{2,1,0:T(1,128)S(1)}, u32[]{:S(2)}, u32[]{:S(2)}) async-start(s32[32,1,16]{2,1,0:T(1,128)} %bitcast.32), calls=%async_computation | async-start | bytes 32768 | tf_op jit(solution)/shard_map/all_to_all | solution.py:165
  213.5 9.3 %all-to-all-done = s32[32,1,16]{2,1,0:T(1,128)S(1)} async-done(((s32[32,1,16]{2,1,0:T(1,128)}), s32[32,1,16]{2,1,0:T(1,128)S(1)}, u32[]{:S(2)}, u32[]{:S(2)}) %all-to-all-start) | async-done | bytes 2080 | tf_op jit(solution)/shard_map/all_to_all | solution.py:165
  223.1 1.9 gather_fusion.2
  225.0 4.1 %all-to-all-start.1 = ((bf16[32,16,1,128]{3,1,2,0:T(8,128)(2,1)}), bf16[32,16,1,128]{3,1,2,0:T(8,128)(2,1)S(1)}, u32[]{:S(2)}, u32[]{:S(2)}) async-start(bf16[32,16,1,128]{3,1,2,0:T(8,128)(2,1)} %bitcast.36), calls=%async_computation.1 | async-start | bytes 262144 | tf_op jit(solution)/shard_map/all_to_all | solution.py:164
  229.8 10.3 %all-to-all-done.1 = bf16[32,16,1,128]{3,1,2,0:T(8,128)(2,1)S(1)} async-done(((bf16[32,16,1,128]{3,1,2,0:T(8,128)(2,1)}), bf16[32,16,1,128]{3,1,2,0:T(8,128)(2,1)S(1)}, u32[]{:S(2)}, u32[]{:S(2)}) %all-to-all-start.1) | async-done | bytes 131104 | tf_op jit(solution)/shard_map/all_to_all | solution.py:164
  240.1 2.4 scatter_custom_fusion
  243.5 1.2 add_convert_fusion
  (95 shorter events, 19.7 us)
Async XLA Ops:
  7.2 76.5 %copy-start = (bf16[192,1536]{1,0:T(8,128)(2,1)S(1)}, bf16[192,1536]{1,0:T(8,128)(2,1)}, u32[]{:S(2)}) copy-start(bf16[192,1536]{1,0:T(8,128)(2,1)} %param.24) | copy-start | bytes 1769476
  7.2 57.7 %copy-start.7 = (s32[512]{0:T(512)S(1)}, s32[512]{0:T(512)}, u32[]{:S(2)}) copy-start(s32[512]{0:T(512)} %param.18) | copy-start | bytes 6148
  7.2 57.7 %copy-start.4 = (s32[512]{0:T(512)S(1)}, s32[512]{0:T(512)}, u32[]{:S(2)}) copy-start(s32[512]{0:T(512)} %param.19) | copy-start | bytes 6148
  7.2 60.8 %all-gather.2.cloned.1.call-start = ((), (), s32[]{:S(2)}) async-start(), calls=%async_computation.3 | async-start | bytes 2211840 | tf_op jit(solution)/shard_map/all_gather | solution.py:110
  8.1 22.0 %collective-permute-start = (bf16[48,320]{1,0:T(8,128)(2,1)S(1)}, bf16[48,320]{1,0:T(8,128)(2,1)S(1)}, u32[]{:S(2)}, u32[]{:S(2)}) collective-permute-start(bf16[48,320]{1,0:T(8,128)(2,1)S(1)} %pad_maximum_fusion.3), channel_id=1, source_target_pairs={{0,32},{32,64},{64,96},{96,128},{128,160},{160,192},{192,224},{224... | collective-permute-start | bytes 92168 | tf_op jit(solution)/shard_map/ppermute | solution.py:76
  10.6 21.9 %collective-permute-start.1 = (bf16[48,320]{1,0:T(8,128)(2,1)S(1)}, bf16[48,320]{1,0:T(8,128)(2,1)S(1)}, u32[]{:S(2)}, u32[]{:S(2)}) collective-permute-start(bf16[48,320]{1,0:T(8,128)(2,1)S(1)} %pad_maximum_fusion.3), channel_id=1, source_target_pairs={{0,64},{32,96},{64,128},{96,160},{128,192},{160,224},{192,0},{224,... | collective-permute-start | bytes 92168 | tf_op jit(solution)/shard_map/ppermute | solution.py:76
  13.6 19.8 %collective-permute-start.2 = (bf16[48,320]{1,0:T(8,128)(2,1)S(1)}, bf16[48,320]{1,0:T(8,128)(2,1)S(1)}, u32[]{:S(2)}, u32[]{:S(2)}) collective-permute-start(bf16[48,320]{1,0:T(8,128)(2,1)S(1)} %pad_maximum_fusion.3), channel_id=1, source_target_pairs={{0,96},{32,128},{64,160},{96,192},{128,224},{160,0},{192,32},{224,... | collective-permute-start | bytes 92168 | tf_op jit(solution)/shard_map/ppermute | solution.py:76
  17.4 17.0 %collective-permute-start.3 = (bf16[48,320]{1,0:T(8,128)(2,1)S(1)}, bf16[48,320]{1,0:T(8,128)(2,1)S(1)}, u32[]{:S(2)}, u32[]{:S(2)}) collective-permute-start(bf16[48,320]{1,0:T(8,128)(2,1)S(1)} %pad_maximum_fusion.3), channel_id=1, source_target_pairs={{0,128},{32,160},{64,192},{96,224},{128,0},{160,32},{192,64},{224,... | collective-permute-start | bytes 92168 | tf_op jit(solution)/shard_map/ppermute | solution.py:76
  21.0 157.2 %all-reduce.3.cloned.1.call-start = ((), (), s32[]{:S(2)}) async-start(), calls=%async_computation.4 | async-start | bytes 6291456 | tf_op jit(solution)/shard_map/psum | solution.py:144
  21.1 3.6 %collective-permute-start.10 = (s32[512]{0:T(512)}, s32[512]{0:T(512)S(1)}, u32[]{:S(2)}, u32[]{:S(2)}) collective-permute-start(s32[512]{0:T(512)} %param.18), channel_id=1, source_target_pairs={{0,8},{8,0},{1,9},{9,1},{2,10},{10,2},{3,11},{11,3},{4,12},{12,4},... | collective-permute-start | bytes 6152 | tf_op jit(solution)/shard_map/ppermute | solution.py:132
  24.7 9.7 %collective-permute-start.4 = (bf16[48,320]{1,0:T(8,128)(2,1)S(1)}, bf16[48,320]{1,0:T(8,128)(2,1)S(1)}, u32[]{:S(2)}, u32[]{:S(2)}) collective-permute-start(bf16[48,320]{1,0:T(8,128)(2,1)S(1)} %pad_maximum_fusion.3), channel_id=1, source_target_pairs={{0,160},{32,192},{64,224},{96,0},{128,32},{160,64},{192,96},{224,1... | collective-permute-start | bytes 92168 | tf_op jit(solution)/shard_map/ppermute | solution.py:76
  30.1 4.5 %collective-permute-start.5 = (bf16[48,320]{1,0:T(8,128)(2,1)S(1)}, bf16[48,320]{1,0:T(8,128)(2,1)S(1)}, u32[]{:S(2)}, u32[]{:S(2)}) collective-permute-start(bf16[48,320]{1,0:T(8,128)(2,1)S(1)} %pad_maximum_fusion.3), channel_id=1, source_target_pairs={{0,192},{32,224},{64,0},{96,32},{128,64},{160,96},{192,128},{224,1... | collective-permute-start | bytes 92168 | tf_op jit(solution)/shard_map/ppermute | solution.py:76
  32.6 2.9 %collective-permute-start.6 = (bf16[48,320]{1,0:T(8,128)(2,1)S(1)}, bf16[48,320]{1,0:T(8,128)(2,1)S(1)}, u32[]{:S(2)}, u32[]{:S(2)}) collective-permute-start(bf16[48,320]{1,0:T(8,128)(2,1)S(1)} %pad_maximum_fusion.3), channel_id=1, source_target_pairs={{0,224},{32,0},{64,32},{96,64},{128,96},{160,128},{192,160},{224,1... | collective-permute-start | bytes 92168 | tf_op jit(solution)/shard_map/ppermute | solution.py:76
  33.4 5.8 %collective-permute-start.11 = (s32[512]{0:T(512)}, s32[512]{0:T(512)S(1)}, u32[]{:S(2)}, u32[]{:S(2)}) collective-permute-start(s32[512]{0:T(512)} %param.19), channel_id=1, source_target_pairs={{0,8},{8,0},{1,9},{9,1},{2,10},{10,2},{3,11},{11,3},{4,12},{12,4},... | collective-permute-start | bytes 6152 | tf_op jit(solution)/shard_map/ppermute | solution.py:132
  36.2 27.7 %collective-permute-start.7 = (bf16[8,48,320]{2,1,0:T(8,128)(2,1)S(1)}, bf16[8,48,320]{2,1,0:T(8,128)(2,1)S(1)}, u32[]{:S(2)}, u32[]{:S(2)}) collective-permute-start(bf16[8,48,320]{2,1,0:T(8,128)(2,1)S(1)} %broadcast_select_fusion), channel_id=1, source_target_pairs={{0,16},{16,0},{1,17},{17,1},{2,18},{18,2},{3,19},{19,3},{4,20},{20... | collective-permute-start | bytes 737288 | tf_op jit(solution)/shard_map/ppermute | solution.py:80
  64.1 2.4 collective-permute-start.8
  72.3 4.3 %copy-start.3 = (bf16[8,2,2,48,320]{4,3,2,1,0:T(8,128)(2,1)S(1)}, bf16[8,2,2,48,320]{4,3,2,1,0:T(8,128)(2,1)}, u32[]{:S(2)}) copy-start(bf16[8,2,2,48,320]{4,3,2,1,0:T(8,128)(2,1)} %copy.50) | copy-start | bytes 2949124
  77.5 1.4 collective-permute-start.9
  83.7 2.7 %copy-start.5 = (f32[512,8]{0,1:T(8,128)S(1)}, f32[512,8]{0,1:T(8,128)}, u32[]{:S(2)}) copy-start(f32[512,8]{0,1:T(8,128)} %param.26) | copy-start | bytes 49156
  83.7 2.7 %copy-start.6 = (s32[512,8]{0,1:T(8,128)S(1)}, s32[512,8]{0,1:T(8,128)}, u32[]{:S(2)}) copy-start(s32[512,8]{0,1:T(8,128)} %param.25) | copy-start | bytes 49156
  86.0 156.4 %reduce-scatter.4.cloned.1.call-start = ((), (), s32[]{:S(2)}) async-start(), calls=%async_computation.5 | async-start | bytes 1769472
  180.6 7.6 %copy-start.2 = (bf16[512,1536]{1,0:T(8,128)(2,1)}, bf16[512,1536]{1,0:T(8,128)(2,1)S(1)}, u32[]{:S(2)}) copy-start(bf16[512,1536]{1,0:T(8,128)(2,1)S(1)} %get-tuple-element.47) | copy-start | bytes 4718596
  180.6 7.6 %copy-start.8 = (bf16[5,256,1536]{2,1,0:T(8,128)(2,1)S(1)}, bf16[5,256,1536]{2,1,0:T(8,128)(2,1)}, u32[]{:S(2)}) copy-start(bf16[5,256,1536]{2,1,0:T(8,128)(2,1)} %param.28) | copy-start | bytes 11796484
  191.7 1.6 copy-start.1
  201.3 21.6 %all-to-all-start = ((s32[32,1,16]{2,1,0:T(1,128)}), s32[32,1,16]{2,1,0:T(1,128)S(1)}, u32[]{:S(2)}, u32[]{:S(2)}) async-start(s32[32,1,16]{2,1,0:T(1,128)} %bitcast.32), calls=%async_computation | async-start | bytes 32768 | tf_op jit(solution)/shard_map/all_to_all | solution.py:165
  225.0 15.1 %all-to-all-start.1 = ((bf16[32,16,1,128]{3,1,2,0:T(8,128)(2,1)}), bf16[32,16,1,128]{3,1,2,0:T(8,128)(2,1)S(1)}, u32[]{:S(2)}, u32[]{:S(2)}) async-start(bf16[32,16,1,128]{3,1,2,0:T(8,128)(2,1)} %bitcast.36), calls=%async_computation.1 | async-start | bytes 262144 | tf_op jit(solution)/shard_map/all_to_all | solution.py:164
Sparse Core Ops, SparseCore 0:
  21.1 40.3 all-gather.1
  86.2 91.9 all-reduce.2
  193.4 40.6 reduce-scatter.3
where the time goes:
time: 253 us; the launch traced here: 252 us
  waiting for transfers between devices  138 us (55%)
  starting transfers between devices  41.3 us (16%)
  local copies, waits for them, and re-layouts  19.8 us (8%)
  other arithmetic  19.5 us (8%)
  matrix products  19.4 us (8%)
  between operations  14.2 us (6%)
    psum x1, waiting for transfers between devices, shards(): summed = lax.psum(partial_value, T)  91.7 us
    ppermute x1, waiting for transfers between devices, gather_rows_over_groups(): other_y = lax.ppermute(zfull, 'yh', [(0, 1), (1, 0)])  23.9 us
    ppermute x7, starting transfers between devices, gather_rows_over_groups(): got.append(lax.ppermute(block, 'z', [(i, (i + k) % nz) for i in range(nz)]))  17.7 us
    all_to_all x1, starting transfers between devices, shards(): lax.all_to_all(send_slots, G, split_axis=0, concat_axis=0, tiled=True)  12.2 us
    all_to_all x1, waiting for transfers between devices, shards(): lax.all_to_all(send_rows, G, split_axis=0, concat_axis=0, tiled=True)  10.3 us
    all_to_all x1, waiting for transfers between devices, shards(): lax.all_to_all(send_slots, G, split_axis=0, concat_axis=0, tiled=True)  9.3 us
    dot_general x1, matrix products, expert_terms(): jnp.einsum('td,edf->etf', normed, gateup, preferred_element_type=jnp.floa...  7.52 us
    unnamed x28, local copies, waits for them, and re-layouts  5.28 us
  transfers between devices with their start and end apart: 17, of which 8 were waited for; matrix products, arithmetic and copies ran while one was open for 9% of the time, Pallas kernels for 0%

commit v1 on v0

--- a/solution.py
+++ b/solution.py
@@ -141,7 +141,7 @@
     attended = mixed.reshape(tokens, heads_local * HD)
     log_sums = log_part.reshape(heads_local, tokens)
     partial_value = jnp.dot(attended, output_weight, preferred_element_type=jnp.float32)
-    summed = lax.psum(partial_value, T)
+    summed = lax.psum(lax.psum(partial_value, "yl"), "x")
     residual = (states_full.astype(jnp.float32) + summed).astype(jnp.bfloat16)
     normed = rms_scale(residual, gain_forward)
     residual_share = lax.dynamic_slice_in_dim(residual, head_rank * width_share, width_share, 1)

time: 253 us -> 339 us (1.34)
  waiting for transfers between devices: 138 us -> 226 us
    psum x1 -> x2, waiting for transfers between devices: 91.7 us -> 180 us  [shards(): summed = lax.psum(lax.psum(partial_value, 'yl'), 'x')]
  transfers between devices with their start and end apart: 17 -> 18, of which waited for: 8 -> 9; matrix products, arithmetic and copies ran while one was open for 9% -> 7% of each run, Pallas kernels for 0% -> 0%
where the time goes in v1:
time: 339 us
  waiting for transfers between devices  226 us (67%)
  starting transfers between devices  39.3 us (12%)
  local copies, waits for them, and re-layouts  19.8 us (6%)
  other arithmetic  19.5 us (6%)
  matrix products  19.4 us (6%)
  between operations  14.2 us (4%)
    psum x2, waiting for transfers between devices, shards(): summed = lax.psum(lax.psum(partial_value, 'yl'), 'x')  180 us
    ppermute x1, waiting for transfers between devices, gather_rows_over_groups(): other_y = lax.ppermute(zfull, 'yh', [(0, 1), (1, 0)])  23.9 us
    ppermute x7, starting transfers between devices, gather_rows_over_groups(): got.append(lax.ppermute(block, 'z', [(i, (i + k) % nz) for i in range(nz)]))  17.7 us
    all_to_all x1, waiting for transfers between devices, shards(): lax.all_to_all(send_rows, G, split_axis=0, concat_axis=0, tiled=True)  10.3 us
    all_to_all x1, starting transfers between devices, shards(): lax.all_to_all(send_slots, G, split_axis=0, concat_axis=0, tiled=True)  10.3 us
    all_to_all x1, waiting for transfers between devices, shards(): lax.all_to_all(send_slots, G, split_axis=0, concat_axis=0, tiled=True)  9.28 us
    dot_general x1, matrix products, expert_terms(): jnp.einsum('td,edf->etf', normed, gateup, preferred_element_type=jnp.floa...  7.52 us
  transfers between devices with their start and end apart: 18, of which 9 were waited for; matrix products, arithmetic and copies ran while one was open for 7% of the time, Pallas kernels for 0%

profile of v1, /device:TPU:1, one launch (start us, length us, event | category | flops | bytes accessed | tf_op | source)
XLA Modules:
  0.0 338.6 jit_solution(17400424234452786698)
XLA Ops:
  8.1 2.5 collective-permute-start
  10.6 3.0 collective-permute-start.1
  13.6 3.8 %collective-permute-start.2 = (bf16[48,320]{1,0:T(8,128)(2,1)S(1)}, bf16[48,320]{1,0:T(8,128)(2,1)S(1)}, u32[]{:S(2)}, u32[]{:S(2)}) collective-permute-start(bf16[48,320]{1,0:T(8,128)(2,1)S(1)} %pad_maximum_fusion.3), channel_id=1, source_target_pairs={{0,96},{32,128},{64,160},{96,192},{128,224},{160,0},{192,32},{224,... | collective-permute-start | bytes 92168 | tf_op jit(solution)/shard_map/ppermute | solution.py:76
  19.3 1.7 pad_maximum_fusion.1
  21.1 1.7 collective-permute-start.10
  24.7 4.7 %collective-permute-start.4 = (bf16[48,320]{1,0:T(8,128)(2,1)S(1)}, bf16[48,320]{1,0:T(8,128)(2,1)S(1)}, u32[]{:S(2)}, u32[]{:S(2)}) collective-permute-start(bf16[48,320]{1,0:T(8,128)(2,1)S(1)} %pad_maximum_fusion.3), channel_id=1, source_target_pairs={{0,160},{32,192},{64,224},{96,0},{128,32},{160,64},{192,96},{224,1... | collective-permute-start | bytes 92168 | tf_op jit(solution)/shard_map/ppermute | solution.py:76
  30.1 2.5 collective-permute-start.5
  36.2 3.0 collective-permute-start.7
  40.0 23.9 %collective-permute-done.7 = bf16[8,48,320]{2,1,0:T(8,128)(2,1)S(1)} collective-permute-done((bf16[8,48,320]{2,1,0:T(8,128)(2,1)S(1)}, bf16[8,48,320]{2,1,0:T(8,128)(2,1)S(1)}, u32[]{:S(2)}, u32[]{:S(2)}) %collective-permute-start.7) | collective-permute-done | bytes 245792 | tf_op jit(solution)/shard_map/ppermute | solution.py:80
  68.0 2.6 slice.95
  70.6 1.7 copy.59
  72.7 1.5 convert_reduce_fusion
  74.3 2.0 convolution_bitcast_fusion.1
  78.9 1.3 fusion.1
  80.2 1.4 fusion
  81.6 2.0 fusion.19
  83.7 2.3 fusion.54
  86.1 96.2 %all-reduce.4.cloned.1.call-done = f32[512,1536]{1,0:T(8,128)} async-done(((f32[512,1536]{1,0:T(8,128)}), f32[512,1536]{1,0:T(8,128)}) %all-reduce.4.cloned.1.call-update) | async-done | bytes 3145744 | tf_op jit(solution)/shard_map/psum | solution.py:144
  182.7 83.9 %all-reduce.6.cloned.1.call-done = f32[512,1536]{1,0:T(8,128)} async-done(((f32[512,1536]{1,0:T(8,128)}), f32[512,1536]{1,0:T(8,128)}) %all-reduce.6.cloned.1.call-update) | async-done | bytes 3145744 | tf_op jit(solution)/shard_map/psum | solution.py:144
  266.7 2.4 fusion.2
  269.1 7.5 %convolution_bitcast_fusion = f32[5,512,512]{2,1,0:T(8,128)S(1)} fusion(bf16[5,1536,512]{2,1,0:T(8,128)(2,1)} %param.27, bf16[512,1536]{1,0:T(8,128)(2,1)S(1)} %get-tuple-element.47, f32[1536]{0:T(1024)S(1)} %get-tuple-element.44, f32[512]{0:T(512)S(1)} %add_rsqrt_fusion), kind=kOutput, calls=%fused_computation.26 | convolution fusion | flops 4029677568 | bytes 14688256 | tf_op jit(solution)/shard_map/td,edf->etf/dot_general | solution.py:62
  276.7 3.5 %multiply_reduce_fusion = bf16[512,1536]{1,0:T(8,128)(2,1)S(1)} fusion(bf16[5,256,1536]{2,1,0:T(8,128)(2,1)S(1)} %copy-done.8, f32[5,512]{1,0:T(8,128)S(1)} %bitcast.103, f32[5,512,512]{2,1,0:T(8,128)S(1)} %convolution_bitcast_fusion), kind=kOutput, calls=%fused_computation.4 | convolution fusion | flops 2024275968 | bytes 10758144 | tf_op jit(solution)/shard_map/etf,efd->etd/dot_general | solution.py:66
  280.2 1.6 copy.57
  281.8 3.8 %sort.17 = (s32[512]{0:T(512)}, s32[512]{0:T(512)S(1)}) sort(s32[512]{0:T(512)S(1)} %fusion.43, s32[512]{0:T(512)S(1)} %iota.31), dimensions={0}, to_apply=%region_9.10 | sort | flops 4608 | bytes 8192 | tf_op jit(solution)/shard_map/jit(argsort)/sort | solution.py:160
  285.6 3.5 %gather_fusion.1 = s32[512]{0:T(512)S(1)} fusion(s32[512]{0:T(512)S(1)} %copy-done.1, s32[1024]{0:T(1024)S(1)} %pad_clamp_fusion), kind=kCustom, calls=%fused_computation.1 | custom fusion | bytes 6144 | tf_op jit(solution)/shard_map/gather | solution.py:162
  289.8 10.3 %all-to-all-start = ((s32[32,1,16]{2,1,0:T(1,128)}), s32[32,1,16]{2,1,0:T(1,128)S(1)}, u32[]{:S(2)}, u32[]{:S(2)}) async-start(s32[32,1,16]{2,1,0:T(1,128)} %bitcast.32), calls=%async_computation | async-start | bytes 32768 | tf_op jit(solution)/shard_map/all_to_all | solution.py:165
  300.1 9.3 %all-to-all-done = s32[32,1,16]{2,1,0:T(1,128)S(1)} async-done(((s32[32,1,16]{2,1,0:T(1,128)}), s32[32,1,16]{2,1,0:T(1,128)S(1)}, u32[]{:S(2)}, u32[]{:S(2)}) %all-to-all-start) | async-done | bytes 2080 | tf_op jit(solution)/shard_map/all_to_all | solution.py:165
  309.6 1.9 gather_fusion.2
  311.5 4.1 %all-to-all-start.1 = ((bf16[32,16,1,128]{3,1,2,0:T(8,128)(2,1)}), bf16[32,16,1,128]{3,1,2,0:T(8,128)(2,1)S(1)}, u32[]{:S(2)}, u32[]{:S(2)}) async-start(bf16[32,16,1,128]{3,1,2,0:T(8,128)(2,1)} %bitcast.36), calls=%async_computation.1 | async-start | bytes 262144 | tf_op jit(solution)/shard_map/all_to_all | solution.py:164
  316.3 10.3 %all-to-all-done.1 = bf16[32,16,1,128]{3,1,2,0:T(8,128)(2,1)S(1)} async-done(((bf16[32,16,1,128]{3,1,2,0:T(8,128)(2,1)}), bf16[32,16,1,128]{3,1,2,0:T(8,128)(2,1)S(1)}, u32[]{:S(2)}, u32[]{:S(2)}) %all-to-all-start.1) | async-done | bytes 131104 | tf_op jit(solution)/shard_map/all_to_all | solution.py:164
  326.6 2.4 scatter_custom_fusion
  330.1 1.2 add_convert_fusion
  (98 shorter events, 20.9 us)
Async XLA Ops:
  7.2 76.5 %copy-start = (bf16[192,1536]{1,0:T(8,128)(2,1)S(1)}, bf16[192,1536]{1,0:T(8,128)(2,1)}, u32[]{:S(2)}) copy-start(bf16[192,1536]{1,0:T(8,128)(2,1)} %param.24) | copy-start | bytes 1769476
  7.2 57.7 %copy-start.7 = (s32[512]{0:T(512)S(1)}, s32[512]{0:T(512)}, u32[]{:S(2)}) copy-start(s32[512]{0:T(512)} %param.18) | copy-start | bytes 6148
  7.2 57.7 %copy-start.4 = (s32[512]{0:T(512)S(1)}, s32[512]{0:T(512)}, u32[]{:S(2)}) copy-start(s32[512]{0:T(512)} %param.19) | copy-start | bytes 6148
  7.2 60.8 %all-gather.2.cloned.1.call-start = ((), (), s32[]{:S(2)}) async-start(), calls=%async_computation.3 | async-start | bytes 2211840 | tf_op jit(solution)/shard_map/all_gather | solution.py:110
  8.1 22.0 %collective-permute-start = (bf16[48,320]{1,0:T(8,128)(2,1)S(1)}, bf16[48,320]{1,0:T(8,128)(2,1)S(1)}, u32[]{:S(2)}, u32[]{:S(2)}) collective-permute-start(bf16[48,320]{1,0:T(8,128)(2,1)S(1)} %pad_maximum_fusion.3), channel_id=1, source_target_pairs={{0,32},{32,64},{64,96},{96,128},{128,160},{160,192},{192,224},{224... | collective-permute-start | bytes 92168 | tf_op jit(solution)/shard_map/ppermute | solution.py:76
  10.6 21.9 %collective-permute-start.1 = (bf16[48,320]{1,0:T(8,128)(2,1)S(1)}, bf16[48,320]{1,0:T(8,128)(2,1)S(1)}, u32[]{:S(2)}, u32[]{:S(2)}) collective-permute-start(bf16[48,320]{1,0:T(8,128)(2,1)S(1)} %pad_maximum_fusion.3), channel_id=1, source_target_pairs={{0,64},{32,96},{64,128},{96,160},{128,192},{160,224},{192,0},{224,... | collective-permute-start | bytes 92168 | tf_op jit(solution)/shard_map/ppermute | solution.py:76
  13.6 19.8 %collective-permute-start.2 = (bf16[48,320]{1,0:T(8,128)(2,1)S(1)}, bf16[48,320]{1,0:T(8,128)(2,1)S(1)}, u32[]{:S(2)}, u32[]{:S(2)}) collective-permute-start(bf16[48,320]{1,0:T(8,128)(2,1)S(1)} %pad_maximum_fusion.3), channel_id=1, source_target_pairs={{0,96},{32,128},{64,160},{96,192},{128,224},{160,0},{192,32},{224,... | collective-permute-start | bytes 92168 | tf_op jit(solution)/shard_map/ppermute | solution.py:76
  17.4 17.0 %collective-permute-start.3 = (bf16[48,320]{1,0:T(8,128)(2,1)S(1)}, bf16[48,320]{1,0:T(8,128)(2,1)S(1)}, u32[]{:S(2)}, u32[]{:S(2)}) collective-permute-start(bf16[48,320]{1,0:T(8,128)(2,1)S(1)} %pad_maximum_fusion.3), channel_id=1, source_target_pairs={{0,128},{32,160},{64,192},{96,224},{128,0},{160,32},{192,64},{224,... | collective-permute-start | bytes 92168 | tf_op jit(solution)/shard_map/ppermute | solution.py:76
  21.0 161.3 %all-reduce.4.cloned.1.call-start = ((), (), s32[]{:S(2)}) async-start(), calls=%async_computation.4 | async-start | bytes 6291456 | tf_op jit(solution)/shard_map/psum | solution.py:144
  21.1 3.6 %collective-permute-start.10 = (s32[512]{0:T(512)}, s32[512]{0:T(512)S(1)}, u32[]{:S(2)}, u32[]{:S(2)}) collective-permute-start(s32[512]{0:T(512)} %param.18), channel_id=1, source_target_pairs={{0,8},{8,0},{1,9},{9,1},{2,10},{10,2},{3,11},{11,3},{4,12},{12,4},... | collective-permute-start | bytes 6152 | tf_op jit(solution)/shard_map/ppermute | solution.py:132
  24.7 9.7 %collective-permute-start.4 = (bf16[48,320]{1,0:T(8,128)(2,1)S(1)}, bf16[48,320]{1,0:T(8,128)(2,1)S(1)}, u32[]{:S(2)}, u32[]{:S(2)}) collective-permute-start(bf16[48,320]{1,0:T(8,128)(2,1)S(1)} %pad_maximum_fusion.3), channel_id=1, source_target_pairs={{0,160},{32,192},{64,224},{96,0},{128,32},{160,64},{192,96},{224,1... | collective-permute-start | bytes 92168 | tf_op jit(solution)/shard_map/ppermute | solution.py:76
  30.1 4.5 %collective-permute-start.5 = (bf16[48,320]{1,0:T(8,128)(2,1)S(1)}, bf16[48,320]{1,0:T(8,128)(2,1)S(1)}, u32[]{:S(2)}, u32[]{:S(2)}) collective-permute-start(bf16[48,320]{1,0:T(8,128)(2,1)S(1)} %pad_maximum_fusion.3), channel_id=1, source_target_pairs={{0,192},{32,224},{64,0},{96,32},{128,64},{160,96},{192,128},{224,1... | collective-permute-start | bytes 92168 | tf_op jit(solution)/shard_map/ppermute | solution.py:76
  32.6 2.9 collective-permute-start.6
  33.4 5.8 %collective-permute-start.11 = (s32[512]{0:T(512)}, s32[512]{0:T(512)S(1)}, u32[]{:S(2)}, u32[]{:S(2)}) collective-permute-start(s32[512]{0:T(512)} %param.19), channel_id=1, source_target_pairs={{0,8},{8,0},{1,9},{9,1},{2,10},{10,2},{3,11},{11,3},{4,12},{12,4},... | collective-permute-start | bytes 6152 | tf_op jit(solution)/shard_map/ppermute | solution.py:132
  36.2 27.7 %collective-permute-start.7 = (bf16[8,48,320]{2,1,0:T(8,128)(2,1)S(1)}, bf16[8,48,320]{2,1,0:T(8,128)(2,1)S(1)}, u32[]{:S(2)}, u32[]{:S(2)}) collective-permute-start(bf16[8,48,320]{2,1,0:T(8,128)(2,1)S(1)} %broadcast_select_fusion), channel_id=1, source_target_pairs={{0,16},{16,0},{1,17},{17,1},{2,18},{18,2},{3,19},{19,3},{4,20},{20... | collective-permute-start | bytes 737288 | tf_op jit(solution)/shard_map/ppermute | solution.py:80
  64.1 2.4 collective-permute-start.8
  72.3 4.3 %copy-start.3 = (bf16[8,2,2,48,320]{4,3,2,1,0:T(8,128)(2,1)S(1)}, bf16[8,2,2,48,320]{4,3,2,1,0:T(8,128)(2,1)}, u32[]{:S(2)}) copy-start(bf16[8,2,2,48,320]{4,3,2,1,0:T(8,128)(2,1)} %copy.50) | copy-start | bytes 2949124
  77.5 1.4 collective-permute-start.9
  86.0 96.6 %copy-start.5 = (f32[512,8]{0,1:T(8,128)S(1)}, f32[512,8]{0,1:T(8,128)}, u32[]{:S(2)}) copy-start(f32[512,8]{0,1:T(8,128)} %param.26) | copy-start | bytes 49156
  86.0 96.6 %copy-start.6 = (s32[512,8]{0,1:T(8,128)S(1)}, s32[512,8]{0,1:T(8,128)}, u32[]{:S(2)}) copy-start(s32[512,8]{0,1:T(8,128)} %param.25) | copy-start | bytes 49156
  86.0 180.6 %all-reduce.6.cloned.1.call-start = ((), (), s32[]{:S(2)}) async-start(), calls=%async_computation.5 | async-start | bytes 6291456 | tf_op jit(solution)/shard_map/psum | solution.py:144
  182.3 146.7 %reduce-scatter.4.cloned.1.call-start = ((), (), s32[]{:S(2)}) async-start(), calls=%async_computation.6 | async-start | bytes 1769472
  269.1 7.6 %copy-start.2 = (bf16[512,1536]{1,0:T(8,128)(2,1)}, bf16[512,1536]{1,0:T(8,128)(2,1)S(1)}, u32[]{:S(2)}) copy-start(bf16[512,1536]{1,0:T(8,128)(2,1)S(1)} %get-tuple-element.47) | copy-start | bytes 4718596
  269.1 7.6 %copy-start.8 = (bf16[5,256,1536]{2,1,0:T(8,128)(2,1)S(1)}, bf16[5,256,1536]{2,1,0:T(8,128)(2,1)}, u32[]{:S(2)}) copy-start(bf16[5,256,1536]{2,1,0:T(8,128)(2,1)} %param.28) | copy-start | bytes 11796484
  280.1 1.6 copy-start.1
  289.8 19.6 %all-to-all-start = ((s32[32,1,16]{2,1,0:T(1,128)}), s32[32,1,16]{2,1,0:T(1,128)S(1)}, u32[]{:S(2)}, u32[]{:S(2)}) async-start(s32[32,1,16]{2,1,0:T(1,128)} %bitcast.32), calls=%async_computation | async-start | bytes 32768 | tf_op jit(solution)/shard_map/all_to_all | solution.py:165
  311.5 15.1 %all-to-all-start.1 = ((bf16[32,16,1,128]{3,1,2,0:T(8,128)(2,1)}), bf16[32,16,1,128]{3,1,2,0:T(8,128)(2,1)S(1)}, u32[]{:S(2)}, u32[]{:S(2)}) async-start(bf16[32,16,1,128]{3,1,2,0:T(8,128)(2,1)} %bitcast.36), calls=%async_computation.1 | async-start | bytes 262144 | tf_op jit(solution)/shard_map/all_to_all | solution.py:164
Sparse Core Ops, SparseCore 0:
  21.1 40.3 all-gather.1
  86.1 96.1 all-reduce.3
  184.8 81.8 all-reduce.5
  281.9 38.3 reduce-scatter.3
